TPU v7x, 256 devices: a whole 4x4x8 slice. The times are simulated.
256 devices in a mesh: blk: 16 (over x_lo, y, core), exp: 16 (over z, x_hi).
Axes of the slice: x: 4 (x_hi: 2, x_lo: 2; x = x_hi * 2 + x_lo), y: 4, z: 8, core: 2. Of those that a mesh axis runs over, the one named last changes fastest.
Arguments:
- hidden: bfloat16 [4096, 2560], P('exp', 'blk'), may hold values from -6 to 6
- attn_gain: float32 [2560], replicated, may hold values from 0.25 to 1.75
- qkv_weight: bfloat16 [2560, 3584], P(None, 'blk'), may hold values from -0.125 to 0.125
- out_weight: bfloat16 [2560, 2560], P(None, 'blk'), may hold values from -0.125 to 0.125
- kv_pool: bfloat16 [16, 64, 128, 1024], P('exp', 'blk'), may hold values from -64 to 64
- page_table: int32 [16, 64], P('exp'), may hold values from 0 to 63, each once within a row
- cache_lens: int32 [16], P('exp'), may hold values from 1 to 7936, as said below
- ffn_gain: float32 [2560], replicated, may hold values from 0.25 to 1.75
- route_ids: int32 [4096, 6], P('exp'), may hold values from 0 to 63, all different within a row; in each aligned block of 256 rows (0 to 255, 256 to 511, ...) at most 32 rows name the same one
- route_weights: float32 [4096, 6], P('exp'), may hold values from 0.05 to 2
- shared_gate_up: bfloat16 [2560, 2, 3072], P(None, None, 'blk'), may hold values from -0.125 to 0.125
- shared_down: bfloat16 [3072, 2560], P('blk'), may hold values from -0.109375 to 0.109375
- expert_gate_up: bfloat16 [256, 2560, 768], P(('blk', 'exp')), may hold values from -0.125 to 0.125
- expert_down: bfloat16 [256, 384, 2560], P(('blk', 'exp')), may hold values from -0.3125 to 0.3125
Outputs:
- hidden_out: bfloat16 [4096, 2560], P('exp', 'blk')
- kv_pool_out: bfloat16 [16, 64, 128, 1024], P('exp', 'blk')
Inputs may be any that keep to these rules, and one draw needn't show every extreme that they name: `route_ids`: among the 256 tokens of one request at most 32 choose any one expert, and some expert is chosen by exactly 32 of them; a token's 6 experts differ. `page_table`: each row names every page of the request's pool once. `cache_lens`: some request has exactly 7936 cached tokens.
All inputs are finite; a program needn't handle non-finite values.
Results may differ from a plain program's by a relative error of at most 0.02.
The roundings to bfloat16 on the way count: a program that leaves them out, or rounds other values in their place, can miss the bound.
Values may be sent and summed in bfloat16 or wider, within the bound.
No kernel may reach another device: no remote copies, remote signals or barrier semaphores. Data moves between devices by JAX's collectives and lax.ppermute only.
A program may use at most 256 MiB of HBM per device.

v0:
```python
import math
import jax
import jax.numpy as jnp
from jax import lax
from jax.sharding import PartitionSpec as P

HEADS = 20
KV_HEADS = 4
HEAD_DIM = 128
TOPK = 6
SPLIT = 4
PAGE = 128
NEW = 256
FF_PART = 384
rope_base = 500000.0
norm_eps = 1e-05


def normalize(inputs, gain_vec):
    values = inputs.astype(jnp.float32)
    inv_rms = lax.rsqrt(jnp.mean(values * values, axis=-1, keepdims=True) + norm_eps)
    return (values * inv_rms * gain_vec).astype(jnp.bfloat16)


def rotate(inputs, positions):
    half_dim = HEAD_DIM // 2
    frequency = rope_base ** (-(jnp.arange(half_dim).astype(jnp.float32) * 2.0 / HEAD_DIM))
    angles = positions.astype(jnp.float32)[:, None] * frequency[None, :]
    cosine = jnp.cos(angles)[:, None, :]
    sine_vals = jnp.sin(angles)[:, None, :]
    lower_half = inputs[..., :half_dim]
    upper_half = inputs[..., half_dim:]
    return jnp.concatenate(
        [
            lower_half * cosine - upper_half * sine_vals,
            upper_half * cosine + lower_half * sine_vals,
        ],
        axis=-1,
    )


def partial_softmax(queries, query_pos, block_rows, key_pos):
    key_width = KV_HEADS * HEAD_DIM
    key_rows = block_rows[:, :key_width].reshape(-1, KV_HEADS, HEAD_DIM)
    value_rows = block_rows[:, key_width:].reshape(-1, KV_HEADS, HEAD_DIM)
    scores = jnp.einsum("tkgd,skd->tkgs", queries, key_rows, preferred_element_type=jnp.float32) * (
        1.0 / math.sqrt(HEAD_DIM)
    )
    allowed = (key_pos[None, :] <= query_pos[:, None])[:, None, None, :]
    maxima = jnp.max(jnp.where(allowed, scores, -1e30), axis=-1)
    weights = jnp.where(allowed, jnp.exp(scores - maxima[..., None]), 0.0)
    totals = jnp.sum(weights, axis=-1)
    weighted = jnp.einsum(
        "tkgs,skd->tkgd",
        weights.astype(jnp.bfloat16),
        value_rows,
        preferred_element_type=jnp.float32,
    )
    return (maxima, totals, weighted)


def per_device(
    hidden,
    attn_gain,
    qkv_weight,
    out_weight,
    kv_pool,
    page_table,
    cache_lens,
    ffn_gain,
    route_ids,
    route_weights,
    shared_gate_up,
    shared_down,
    expert_gate_up,
    expert_down,
):
    blocks = lax.axis_size("blk")
    groups = lax.axis_size("exp")
    block_index = lax.axis_index("blk")
    model_width = hidden.shape[1] * blocks
    query_width = HEADS * HEAD_DIM
    key_width = KV_HEADS * HEAD_DIM
    group_size = HEADS // KV_HEADS
    own_rows = NEW // blocks
    full_rows = lax.all_gather(hidden, "blk", axis=1, tiled=True)
    attn_in = normalize(full_rows, attn_gain)
    projected = jnp.dot(attn_in, qkv_weight, preferred_element_type=jnp.float32).astype(
        jnp.bfloat16
    )
    projected_all = lax.all_gather(projected, "blk", axis=1, tiled=True)
    length = cache_lens[0]
    positions = length + jnp.arange(NEW, dtype=jnp.int32)
    queries = rotate(
        projected_all[:, :query_width].astype(jnp.float32).reshape(NEW, HEADS, HEAD_DIM), positions
    ).astype(jnp.bfloat16)
    fresh_keys = rotate(
        projected_all[:, query_width : query_width + key_width]
        .astype(jnp.float32)
        .reshape(NEW, KV_HEADS, HEAD_DIM),
        positions,
    ).astype(jnp.bfloat16)
    appended = jnp.concatenate(
        [fresh_keys.reshape(NEW, key_width), projected_all[:, query_width + key_width :]], axis=1
    )
    page_map = page_table[0]
    pool_pages = page_map.shape[0]
    page_index = jnp.arange(pool_pages, dtype=jnp.int32)
    logical = jnp.sum(
        jnp.where(page_map[None, :] == page_index[:, None], page_index[None, :], 0), axis=1
    )
    local_pages = kv_pool.shape[1]
    local_logical = lax.dynamic_slice_in_dim(logical, block_index * local_pages, local_pages)
    slot_offsets = jnp.arange(PAGE, dtype=jnp.int32)
    local_pos = local_logical[:, None] * PAGE + slot_offsets[None, :]
    offset = local_pos - length
    written = (offset >= 0) & (offset < NEW)
    picked = appended[jnp.clip(offset, 0, NEW - 1)]
    pool_out = jnp.where(written[:, :, None], picked, kv_pool[0])
    grouped = queries.reshape(NEW, KV_HEADS, group_size, HEAD_DIM)
    slot_rows = pool_out.reshape(local_pages * PAGE, 2 * key_width)
    maxima, totals, weighted = partial_softmax(grouped, positions, slot_rows, local_pos.reshape(-1))
    payload = jnp.concatenate(
        [
            weighted.reshape(NEW, query_width),
            maxima.reshape(NEW, HEADS),
            totals.reshape(NEW, HEADS),
        ],
        axis=1,
    ).reshape(blocks, own_rows, query_width + 2 * HEADS)
    gathered = lax.all_to_all(payload, "blk", split_axis=0, concat_axis=0, tiled=True)
    part_acc = gathered[:, :, :query_width].reshape(blocks, own_rows, HEADS, HEAD_DIM)
    part_max = gathered[:, :, query_width : query_width + HEADS]
    part_sum = gathered[:, :, query_width + HEADS :]
    overall = jnp.max(part_max, axis=0)
    factors = jnp.exp(part_max - overall[None])
    total_sum = jnp.sum(part_sum * factors, axis=0)
    total_acc = jnp.sum(part_acc * factors[..., None], axis=0)
    own_attention = (
        (total_acc / total_sum[..., None]).reshape(own_rows, query_width).astype(jnp.bfloat16)
    )
    attended = jnp.dot(
        lax.all_gather(own_attention, "blk", axis=0, tiled=True),
        out_weight,
        preferred_element_type=jnp.float32,
    )
    mixed_cols = (hidden.astype(jnp.float32) + attended).astype(jnp.bfloat16)
    mixed_rows = lax.all_gather(mixed_cols, "blk", axis=1, tiled=True)
    ffn_in = normalize(mixed_rows, ffn_gain)
    shared_cols = shared_gate_up.shape[2]
    gate_up = jnp.dot(
        ffn_in,
        shared_gate_up.reshape(model_width, 2 * shared_cols),
        preferred_element_type=jnp.float32,
    )
    shared_act = (jax.nn.silu(gate_up[:, :shared_cols]) * gate_up[:, shared_cols:]).astype(
        jnp.bfloat16
    )
    shared_term = jnp.dot(shared_act, shared_down, preferred_element_type=jnp.float32)
    row_experts = groups // SPLIT
    expert_count = row_experts * blocks
    capacity = NEW * TOPK * 4 // (expert_count * 3)
    row_expert_ids = block_index * row_experts + jnp.arange(row_experts, dtype=jnp.int32)
    route_hits = route_ids[:, :, None] == row_expert_ids[None, None, :]
    chosen = jnp.any(route_hits, axis=1)
    route_share = jnp.sum(jnp.where(route_hits, route_weights[:, :, None], 0.0), axis=1)
    slot_rank = jnp.cumsum(chosen.astype(jnp.int32), axis=0) - 1
    slot_ids = jnp.arange(capacity, dtype=jnp.int32)
    placed = chosen.T[:, None, :] & (slot_rank.T[:, None, :] == slot_ids[None, :, None])
    selector = placed.astype(jnp.bfloat16)
    outgoing = jnp.einsum(
        "ect,td->ecd", selector, ffn_in, preferred_element_type=jnp.float32
    ).astype(jnp.bfloat16)
    outgoing = jnp.repeat(outgoing, SPLIT, axis=0)
    received = lax.all_to_all(outgoing, "exp", split_axis=0, concat_axis=0, tiled=True)
    flat_rows = received.reshape(-1, model_width)
    expert_gu = jnp.dot(flat_rows, expert_gate_up[0], preferred_element_type=jnp.float32)
    activated = (jax.nn.silu(expert_gu[:, :FF_PART]) * expert_gu[:, FF_PART:]).astype(jnp.bfloat16)
    result = jnp.dot(activated, expert_down[0], preferred_element_type=jnp.float32).astype(
        jnp.bfloat16
    )
    returned = lax.all_to_all(
        result.reshape(received.shape), "exp", split_axis=0, concat_axis=0, tiled=True
    )
    summed = jnp.sum(
        returned.reshape(row_experts, SPLIT, capacity, model_width).astype(jnp.float32), axis=1
    )
    slot_weight = jnp.sum(placed.astype(jnp.float32) * route_share.T[:, None, :], axis=2)
    slot_values = summed * slot_weight[:, :, None]
    upper_part = slot_values.astype(jnp.bfloat16)
    lower_part = (slot_values - upper_part.astype(jnp.float32)).astype(jnp.bfloat16)
    routed = jnp.einsum(
        "ect,ecd->td", selector, upper_part, preferred_element_type=jnp.float32
    ) + jnp.einsum("ect,ecd->td", selector, lower_part, preferred_element_type=jnp.float32)
    layer_term = shared_term + routed
    summed_cols = lax.psum_scatter(layer_term, "blk", scatter_dimension=1, tiled=True)
    hidden_out = (mixed_cols.astype(jnp.float32) + summed_cols).astype(jnp.bfloat16)
    return (hidden_out, pool_out[None])


def solution(mesh):
    placed = (
        P("exp", "blk"),
        P(),
        P(None, "blk"),
        P(None, "blk"),
        P("exp", "blk", None, None),
        P("exp", None),
        P("exp"),
        P(),
        P("exp", None),
        P("exp", None),
        P(None, None, "blk"),
        P("blk", None),
        P(("blk", "exp"), None, None),
        P(("blk", "exp"), None, None),
    )
    return jax.shard_map(
        per_device,
        mesh=mesh,
        in_specs=placed,
        out_specs=(P("exp", "blk"), P("exp", "blk", None, None)),
        check_vma=False,
    )
```

profile of v0, /device:TPU:4, one launch (start us, length us, event | category | flops | bytes accessed | tf_op | source)
XLA Modules:
  0.0 493.9 jit_solution(17672671257017205096)
XLA Ops:
  8.0 40.1 %all-gather.5.cloned.1.call-done = bf16[256,2560]{0,1:T(8,128)(2,1)} async-done(((bf16[256,160]{0,1:T(8,128)(2,1)}), bf16[256,2560]{0,1:T(8,128)(2,1)}) %all-gather.5.cloned.1.call-update) | async-done | bytes 1310736 | tf_op jit(solution)/shard_map/all_gather | solution.py:86
  49.8 3.0 fusion.34
  55.0 34.1 %all-gather.7.cloned.1.call-done = bf16[256,3584]{0,1:T(8,128)(2,1)} async-done(((bf16[256,224]{0,1:T(8,128)(2,1)}), bf16[256,3584]{0,1:T(8,128)(2,1)}) %all-gather.7.cloned.1.call-update) | async-done | bytes 1835024 | tf_op jit(solution)/shard_map/all_gather | solution.py:91
  90.6 2.1 gather_fusion
  99.6 2.3 copy.59
  101.9 2.3 copy.60
  104.2 8.8 %fusion = (f32[256,4,5]{0,2,1:T(8,128)}, f32[4,512,256,5]{2,1,3,0:T(8,128)}) fusion(pred[256,512]{0,1:T(8,128)(4,1)} %broadcast_compare_fusion, bf16[512,4,128,1]{0,2,3,1:T(8,128)(2,1)S(1)} %bitcast.103, bf16[256,4,5,64]{3,0,2,1:T(8,128)(2,1)} %bitcast.101, bf16[256,4,5,64]{3,0,2,1:T(8,128)(2,1)} %bitcast.100), kind=kOutput, calls=%fused_computation.3 | convolution fusion | flops 681569280 | bytes 12472320 | tf_op jit(solution)/shard_map/tkgd,skd->tkgs/dot_general | solution.py:46
  113.9 6.1 %fusion.3 = f32[256,4,5]{0,2,1:T(8,128)S(1)} fusion(f32[4,512,256,5]{2,1,3,0:T(8,128)} %get-tuple-element.15, f32[256,4,5]{0,2,1:T(8,128)} %get-tuple-element.14, pred[256,512]{0,1:T(8,128)(4,1)} %broadcast_compare_fusion), kind=kLoop, calls=%fused_computation.6 | loop fusion | flops 10480640 | bytes 10657792 | tf_op jit(solution)/shard_map/reduce_sum | solution.py:52
  121.0 2.0 copy.57
  123.0 7.8 %fusion.22 = f32[256,4,5,128]{0,3,2,1:T(8,128)} fusion(bf16[512,4,128,1]{0,2,3,1:T(8,128)(2,1)} %bitcast.109, f32[4,512,256,5]{2,1,3,0:T(8,128)} %get-tuple-element.15, f32[256,4,5]{0,2,1:T(8,128)S(1)} %copy-done.11, pred[256,512]{0,1:T(8,128)(4,1)S(1)} %copy-done.2), kind=kOutput, calls=%fused_computation.35 | convolution fusion | flops 681574400 | bytes 13783040 | tf_op jit(solution)/shard_map/tkgs,skd->tkgd/dot_general | solution.py:53
  130.9 5.1 %copy.63 = f32[256,4,5,128]{3,2,1,0:T(8,128)} copy(f32[256,4,5,128]{0,3,2,1:T(8,128)} %fusion.22) | data formatting | bytes 5242880 | tf_op jit(solution)/shard_map/tkgs,skd->tkgd/transpose | solution.py:53
  136.0 4.7 concatenate.31
  140.9 4.0 concatenate.34
  145.0 38.8 %all_to_all.15 = f32[16,16,2600]{2,1,0:T(8,128)S(1)} all-to-all(f32[16,16,2600]{2,1,0:T(8,128)} %concatenate.34), channel_id=1, replica_groups=mesh['blk'=16,'exp'=16] {'blk'}, dimensions={0} | all-to-all | bytes 5324800 | tf_op jit(solution)/shard_map/all_to_all | solution.py:131
  185.5 2.2 mul.210
  187.6 4.2 mul.211
  191.8 2.8 fusion.20
  195.6 34.6 %all-gather.9.cloned.1.call-done = bf16[256,2560]{1,0:T(8,128)(2,1)} async-done(((bf16[16,2560]{1,0:T(8,128)(2,1)}), bf16[256,2560]{1,0:T(8,128)(2,1)}) %all-gather.9.cloned.1.call-update) | async-done | bytes 1310736 | tf_op jit(solution)/shard_map/all_gather | solution.py:143
  230.2 2.7 fusion.37
  234.7 34.0 %all-gather.11.cloned.1.call-done = bf16[256,2560]{0,1:T(8,128)(2,1)} async-done(((bf16[256,160]{0,1:T(8,128)(2,1)}), bf16[256,2560]{0,1:T(8,128)(2,1)}) %all-gather.11.cloned.1.call-update) | async-done | bytes 1310736 | tf_op jit(solution)/shard_map/all_gather | solution.py:148
  268.7 1.7 fusion.17
  270.4 2.0 convolution_convert_fusion.1
  272.7 71.8 %all_to_all.16 = bf16[16,32,2560]{2,1,0:T(8,128)(2,1)S(1)} all-to-all(bf16[16,32,2560]{2,1,0:T(8,128)(2,1)S(1)} %bitcast.98), channel_id=1, replica_groups=mesh['blk'=16,'exp'=16] {'exp'}, dimensions={0} | all-to-all | bytes 5242880 | tf_op jit(solution)/shard_map/all_to_all | solution.py:175
  344.5 2.2 fusion.12
  346.7 3.1 convolution_convert_fusion
  349.8 7.2 %all-to-all-start.2 = ((bf16[16,32,2560]{2,1,0:T(8,128)(2,1)}), bf16[16,32,2560]{2,1,0:T(8,128)(2,1)}, u32[]{:S(2)}, u32[]{:S(2)}) async-start(bf16[16,32,2560]{2,1,0:T(8,128)(2,1)} %bitcast.104), calls=%async_computation.2 | async-start | bytes 5242880 | tf_op jit(solution)/shard_map/all_to_all | solution.py:182
  357.2 3.3 fusion.44
  360.5 55.1 %all-to-all-done.2 = bf16[16,32,2560]{2,1,0:T(8,128)(2,1)} async-done(((bf16[16,32,2560]{2,1,0:T(8,128)(2,1)}), bf16[16,32,2560]{2,1,0:T(8,128)(2,1)}, u32[]{:S(2)}, u32[]{:S(2)}) %all-to-all-start.2) | async-done | bytes 2621472 | tf_op jit(solution)/shard_map/all_to_all | solution.py:182
  415.6 2.3 convert_reduce_fusion
  419.8 2.3 convolution_add_fusion
  422.2 2.4 broadcast_select_fusion
  424.5 61.3 %reduce-scatter.2.cloned.1.call-done = f32[256,160]{0,1:T(8,128)} async-done(((f32[256,2560]{0,1:T(8,128)}), f32[256,160]{0,1:T(8,128)}) %reduce-scatter.2.cloned.1.call-update) | async-done | bytes 163856 | tf_op jit(solution)/shard_map/reduce_scatter | solution.py:196
  (97 shorter events, 22.6 us)
Async XLA Ops:
  7.2 339.5 %copy-start = (bf16[1,384,2560]{2,1,0:T(8,128)(2,1)S(1)}, bf16[1,384,2560]{2,1,0:T(8,128)(2,1)}, u32[]{:S(2)}) copy-start(bf16[1,384,2560]{2,1,0:T(8,128)(2,1)} %param.27) | copy-start | bytes 5898244
  7.2 40.9 %all-gather.5.cloned.1.call-start = ((), (), s32[]{:S(2)}) async-start(), calls=%async_computation.4 | async-start | bytes 1392640 | tf_op jit(solution)/shard_map/all_gather | solution.py:86
  7.9 45.5 %copy-start.16 = (s32[1,64]{1,0:T(1,128)S(1)}, s32[1,64]{1,0:T(1,128)}, u32[]{:S(2)}) copy-start(s32[1,64]{1,0:T(1,128)} %param.19) | copy-start | bytes 772
  7.9 81.2 %all-gather.7.cloned.1.call-start = ((), (), s32[]{:S(2)}) async-start(), calls=%async_computation.5 | async-start | bytes 1949696 | tf_op jit(solution)/shard_map/all_gather | solution.py:91
  52.7 177.5 %all-gather.9.cloned.1.call-start = ((), (), s32[]{:S(2)}) async-start(), calls=%async_computation.6 | async-start | bytes 1392640 | tf_op jit(solution)/shard_map/all_gather | solution.py:143
  54.2 36.1 %copy-start.5 = (f32[256,64]{0,1:T(8,128)}, f32[256,64]{0,1:T(8,128)S(1)}, u32[]{:S(2)}) copy-start(f32[256,64]{0,1:T(8,128)S(1)} %get-tuple-element.12) | copy-start | bytes 196612
  54.2 36.1 %copy-start.7 = (f32[256,64]{0,1:T(8,128)}, f32[256,64]{0,1:T(8,128)S(1)}, u32[]{:S(2)}) copy-start(f32[256,64]{0,1:T(8,128)S(1)} %get-tuple-element.13) | copy-start | bytes 196612
  96.4 1.4 slice-start
  96.4 1.7 copy-start.6
  96.4 1.7 copy-start.8
  113.9 9.2 %copy-start.2 = (pred[256,512]{0,1:T(8,128)(4,1)S(1)}, pred[256,512]{0,1:T(8,128)(4,1)}, u32[]{:S(2)}) copy-start(pred[256,512]{0,1:T(8,128)(4,1)} %broadcast_compare_fusion) | copy-start | bytes 393220
  113.9 9.1 %copy-start.11 = (f32[256,4,5]{0,2,1:T(8,128)S(1)}, f32[256,4,5]{0,2,1:T(8,128)}, u32[]{:S(2)}) copy-start(f32[256,4,5]{0,2,1:T(8,128)} %get-tuple-element.14) | copy-start | bytes 61444
  136.0 4.9 copy-start.9
  183.8 1.6 copy-start.1
  191.8 38.4 %copy-start.10 = (bf16[256,160]{0,1:T(8,128)(2,1)S(1)}, bf16[256,160]{0,1:T(8,128)(2,1)}, u32[]{:S(2)}) copy-start(bf16[256,160]{0,1:T(8,128)(2,1)} %param.14) | copy-start | bytes 245764
  194.7 38.3 %copy-start.12 = (s32[256,6]{0,1:T(8,128)S(1)}, s32[256,6]{0,1:T(8,128)}, u32[]{:S(2)}) copy-start(s32[256,6]{0,1:T(8,128)} %param.22) | copy-start | bytes 18436
  194.7 75.8 %copy-start.15 = (f32[2560]{0:T(1024)S(1)}, f32[2560]{0:T(1024)}, u32[]{:S(2)}) copy-start(f32[2560]{0:T(1024)} %param.21) | copy-start | bytes 30724
  195.5 73.2 %all-gather.11.cloned.1.call-start = ((), (), s32[]{:S(2)}) async-start(), calls=%async_computation.7 | async-start | bytes 1392640 | tf_op jit(solution)/shard_map/all_gather | solution.py:148
  272.7 71.8 %copy-start.14 = (bf16[1,2560,768]{2,1,0:T(8,128)(2,1)S(1)}, bf16[1,2560,768]{2,1,0:T(8,128)(2,1)}, u32[]{:S(2)}) copy-start(bf16[1,2560,768]{2,1,0:T(8,128)(2,1)} %param.26) | copy-start | bytes 11796484
  349.8 7.2 %copy-start.13 = (f32[256,6]{0,1:T(8,128)S(1)}, f32[256,6]{0,1:T(8,128)}, u32[]{:S(2)}) copy-start(f32[256,6]{0,1:T(8,128)} %param.23) | copy-start | bytes 18436
  349.8 65.8 %all-to-all-start.2 = ((bf16[16,32,2560]{2,1,0:T(8,128)(2,1)}), bf16[16,32,2560]{2,1,0:T(8,128)(2,1)}, u32[]{:S(2)}, u32[]{:S(2)}) async-start(bf16[16,32,2560]{2,1,0:T(8,128)(2,1)} %bitcast.104), calls=%async_computation.2 | async-start | bytes 5242880 | tf_op jit(solution)/shard_map/all_to_all | solution.py:182
  356.9 128.9 %reduce-scatter.2.cloned.1.call-start = ((), (), s32[]{:S(2)}) async-start(), calls=%async_computation.8 | async-start | bytes 2785280 | tf_op jit(solution)/shard_map/reduce_scatter | solution.py:196
  418.6 1.2 copy-start.3
  422.0 63.8 %copy-start.4 = (bf16[256,160]{0,1:T(8,128)(2,1)S(1)}, bf16[256,160]{0,1:T(8,128)(2,1)}, u32[]{:S(2)}) copy-start(bf16[256,160]{0,1:T(8,128)(2,1)} %fusion.37) | copy-start | bytes 245764
Sparse Core Ops, SparseCore 0:
  9.9 38.1 all-gather.4
  52.9 36.1 all-gather.6
  195.6 34.5 all-gather.8
  233.1 35.6 all-gather.10
  422.2 63.5 reduce-scatter.1
where the time goes:
time: 495 us; the launch traced here: 494 us
  waiting for transfers between devices  260 us (53%)
  blocking collectives  111 us (22%)
  local copies, waits for them, and re-layouts  38.8 us (8%)
  matrix products  36.3 us (7%)
  other arithmetic  26 us (5%)
  between operations  14.8 us (3%)
  starting transfers between devices  7.37 us (1%)
    all_to_all x1, blocking collectives, per_device(): lax.all_to_all(outgoing, 'exp', split_axis=0, concat_axis=0, tiled=True)  71.8 us
    reduce_scatter x1, waiting for transfers between devices, per_device(): lax.psum_scatter(layer_term, 'blk', scatter_dimension=1, tiled=True)  61.3 us
    all_to_all x1, waiting for transfers between devices, per_device(): lax.all_to_all(result.reshape(received.shape), 'exp', split_axis=0, conca...  55.1 us
    all_gather x1, waiting for transfers between devices, per_device(): full_rows = lax.all_gather(hidden, 'blk', axis=1, tiled=True)  40.1 us
    all_to_all x1, blocking collectives, per_device(): lax.all_to_all(payload, 'blk', split_axis=0, concat_axis=0, tiled=True)  38.8 us
    all_gather x1, waiting for transfers between devices, per_device(): lax.all_gather(own_attention, 'blk', axis=0, tiled=True)  34.6 us
    all_gather x1, waiting for transfers between devices, per_device(): projected_all = lax.all_gather(projected, 'blk', axis=1, tiled=True)  34.1 us
    all_gather x1, waiting for transfers between devices, per_device(): mixed_rows = lax.all_gather(mixed_cols, 'blk', axis=1, tiled=True)  34 us
  transfers between devices with their start and end apart: 6, of which 6 were waited for; matrix products, arithmetic and copies ran while one was open for 2% of the time, Pallas kernels for 0%

commit v1 on v0

--- a/solution.py
+++ b/solution.py
@@ -145,7 +145,8 @@
         preferred_element_type=jnp.float32,
     )
     mixed_cols = (hidden.astype(jnp.float32) + attended).astype(jnp.bfloat16)
-    mixed_rows = lax.all_gather(mixed_cols, "blk", axis=1, tiled=True)
+    sent = jnp.stack([mixed_cols] * lax.axis_size("blk"))
+    mixed_rows = jnp.concatenate(lax.all_to_all(sent, "blk", 0, 0), axis=1)
     ffn_in = normalize(mixed_rows, ffn_gain)
     shared_cols = shared_gate_up.shape[2]
     gate_up = jnp.dot(

time: 495 us -> 477 us (0.964)
  waiting for transfers between devices: 260 us -> 245 us
  matrix products: 36.3 us -> 30.8 us
    all_gather x1 -> x0, waiting for transfers between devices: 34 us -> none  [per_device(): mixed_rows = lax.all_gather(mixed_cols, 'blk', axis=1, tiled=True)]
    all_to_all x0 -> x1, waiting for transfers between devices: none -> 17.7 us  [per_device(): mixed_rows = jnp.concatenate(lax.all_to_all(sent, 'blk', 0, 0), axis=1)]
where the time goes in v1:
time: 477 us; the launch traced here: 476 us
  waiting for transfers between devices  245 us (51%)
  blocking collectives  109 us (23%)
  local copies, waits for them, and re-layouts  39.2 us (8%)
  matrix products  30.8 us (6%)
  other arithmetic  25.9 us (5%)
  between operations  14.8 us (3%)
  starting transfers between devices  11.7 us (2%)
    all_to_all x1, blocking collectives, per_device(): lax.all_to_all(outgoing, 'exp', split_axis=0, concat_axis=0, tiled=True)  70.3 us
    reduce_scatter x1, waiting for transfers between devices, per_device(): lax.psum_scatter(layer_term, 'blk', scatter_dimension=1, tiled=True)  60.9 us
    all_to_all x1, waiting for transfers between devices, per_device(): lax.all_to_all(result.reshape(received.shape), 'exp', split_axis=0, conca...  56.4 us
    all_gather x1, waiting for transfers between devices, per_device(): full_rows = lax.all_gather(hidden, 'blk', axis=1, tiled=True)  40.1 us
    all_to_all x1, blocking collectives, per_device(): lax.all_to_all(payload, 'blk', split_axis=0, concat_axis=0, tiled=True)  38.8 us
    all_gather x1, waiting for transfers between devices, per_device(): lax.all_gather(own_attention, 'blk', axis=0, tiled=True)  34.7 us
    all_gather x1, waiting for transfers between devices, per_device(): projected_all = lax.all_gather(projected, 'blk', axis=1, tiled=True)  34.1 us
    all_to_all x1, waiting for transfers between devices, per_device(): mixed_rows = jnp.concatenate(lax.all_to_all(sent, 'blk', 0, 0), axis=1)  17.7 us
  transfers between devices with their start and end apart: 6, of which 6 were waited for; matrix products, arithmetic and copies ran while one was open for 2% of the time, Pallas kernels for 0%

profile of v1, /device:TPU:4, one launch (start us, length us, event | category | flops | bytes accessed | tf_op | source)
XLA Modules:
  0.0 476.1 jit_solution(7691558595053567446)
XLA Ops:
  8.0 40.1 %all-gather.4.cloned.1.call-done = bf16[256,2560]{0,1:T(8,128)(2,1)} async-done(((bf16[256,160]{0,1:T(8,128)(2,1)}), bf16[256,2560]{0,1:T(8,128)(2,1)}) %all-gather.4.cloned.1.call-update) | async-done | bytes 1310736 | tf_op jit(solution)/shard_map/all_gather | solution.py:86
  48.1 1.7 fusion.14
  49.8 3.0 fusion.33
  55.0 34.1 %all-gather.6.cloned.1.call-done = bf16[256,3584]{0,1:T(8,128)(2,1)} async-done(((bf16[256,224]{0,1:T(8,128)(2,1)}), bf16[256,3584]{0,1:T(8,128)(2,1)}) %all-gather.6.cloned.1.call-update) | async-done | bytes 1835024 | tf_op jit(solution)/shard_map/all_gather | solution.py:91
  90.6 2.1 gather_fusion
  92.6 1.8 bitcast_select_fusion.1
  100.1 1.7 copy.59
  101.8 2.3 copy.60
  104.1 7.9 %fusion = (f32[256,4,5]{0,2,1:T(8,128)S(1)}, f32[4,512,256,5]{2,1,3,0:T(8,128)}) fusion(pred[256,512]{0,1:T(8,128)(4,1)S(1)} %copy-done.4, bf16[512,4,128,1]{0,2,3,1:T(8,128)(2,1)} %bitcast.116, bf16[256,4,5,64]{3,0,2,1:T(8,128)(2,1)} %bitcast.113, bf16[256,4,5,64]{3,0,2,1:T(8,128)(2,1)S(1)} %bitcast.112), kind=kOutput, calls=%fused_computation.3 | convolution fusion | flops 681569280 | bytes 12472320 | tf_op jit(solution)/shard_map/tkgd,skd->tkgs/dot_general | solution.py:46
  112.2 6.1 %fusion.3 = f32[256,4,5]{0,2,1:T(8,128)S(1)} fusion(f32[4,512,256,5]{2,1,3,0:T(8,128)} %get-tuple-element.15, f32[256,4,5]{0,2,1:T(8,128)S(1)} %get-tuple-element.14, pred[256,512]{0,1:T(8,128)(4,1)S(1)} %copy-done.4), kind=kLoop, calls=%fused_computation.6 | loop fusion | flops 10480640 | bytes 10657792 | tf_op jit(solution)/shard_map/reduce_sum | solution.py:52
  119.6 7.8 %fusion.21 = f32[256,4,5,128]{0,3,2,1:T(8,128)} fusion(bf16[512,4,128,1]{0,2,3,1:T(8,128)(2,1)} %bitcast.123, f32[4,512,256,5]{2,1,3,0:T(8,128)} %get-tuple-element.15, f32[256,4,5]{0,2,1:T(8,128)S(1)} %get-tuple-element.14, pred[256,512]{0,1:T(8,128)(4,1)S(1)} %copy-done.4), kind=kOutput, calls=%fused_computation.35 | convolution fusion | flops 681574400 | bytes 13783040 | tf_op jit(solution)/shard_map/tkgs,skd->tkgd/dot_general | solution.py:53
  127.5 5.1 %copy.63 = f32[256,4,5,128]{3,2,1,0:T(8,128)} copy(f32[256,4,5,128]{0,3,2,1:T(8,128)} %fusion.21) | data formatting | bytes 5242880 | tf_op jit(solution)/shard_map/tkgs,skd->tkgd/transpose | solution.py:53
  132.6 4.7 concatenate.31
  137.5 4.0 concatenate.34
  141.5 38.8 %all_to_all.20 = f32[16,16,2600]{2,1,0:T(8,128)S(1)} all-to-all(f32[16,16,2600]{2,1,0:T(8,128)} %concatenate.34), channel_id=1, replica_groups=mesh['blk'=16,'exp'=16] {'blk'}, dimensions={0} | all-to-all | bytes 5324800 | tf_op jit(solution)/shard_map/all_to_all | solution.py:131
  182.0 2.2 mul.228
  184.2 4.2 mul.229
  188.4 2.9 fusion.17
  192.1 34.7 %all-gather.8.cloned.1.call-done = bf16[256,2560]{1,0:T(8,128)(2,1)} async-done(((bf16[16,2560]{1,0:T(8,128)(2,1)}), bf16[256,2560]{1,0:T(8,128)(2,1)}) %all-gather.8.cloned.1.call-update) | async-done | bytes 1310736 | tf_op jit(solution)/shard_map/all_gather | solution.py:143
  226.8 1.9 fusion.36
  229.9 3.9 all-to-all-start.1
  235.6 17.7 %all-to-all-done.1 = bf16[16,256,160]{1,2,0:T(8,128)(2,1)S(1)} async-done(((bf16[16,256,160]{1,2,0:T(8,128)(2,1)}), bf16[16,256,160]{1,2,0:T(8,128)(2,1)S(1)}, u32[]{:S(2)}, u32[]{:S(2)}) %all-to-all-start.1) | async-done | bytes 1310752 | tf_op jit(solution)/shard_map/all_to_all | solution.py:149
  255.0 70.3 %all_to_all.21 = bf16[16,32,2560]{2,1,0:T(8,128)(2,1)S(1)} all-to-all(bf16[16,32,2560]{2,1,0:T(8,128)(2,1)S(1)} %bitcast.110), channel_id=1, replica_groups=mesh['blk'=16,'exp'=16] {'exp'}, dimensions={0} | all-to-all | bytes 5242880 | tf_op jit(solution)/shard_map/all_to_all | solution.py:176
  325.2 2.2 fusion.12
  327.4 3.1 convolution_convert_fusion
  330.5 7.6 %all-to-all-start.3 = ((bf16[16,32,2560]{2,1,0:T(8,128)(2,1)}), bf16[16,32,2560]{2,1,0:T(8,128)(2,1)}, u32[]{:S(2)}, u32[]{:S(2)}) async-start(bf16[16,32,2560]{2,1,0:T(8,128)(2,1)} %bitcast.117), calls=%async_computation.3 | async-start | bytes 5242880 | tf_op jit(solution)/shard_map/all_to_all | solution.py:183
  340.7 56.4 %all-to-all-done.3 = bf16[16,32,2560]{2,1,0:T(8,128)(2,1)} async-done(((bf16[16,32,2560]{2,1,0:T(8,128)(2,1)}), bf16[16,32,2560]{2,1,0:T(8,128)(2,1)}, u32[]{:S(2)}, u32[]{:S(2)}) %all-to-all-start.3) | async-done | bytes 2621472 | tf_op jit(solution)/shard_map/all_to_all | solution.py:183
  397.1 2.3 convert_reduce_fusion
  401.3 2.3 convolution_add_fusion
  404.8 2.4 broadcast_select_fusion
  407.2 60.9 %reduce-scatter.2.cloned.1.call-done = f32[256,160]{0,1:T(8,128)} async-done(((f32[256,2560]{0,1:T(8,128)}), f32[256,160]{0,1:T(8,128)}) %reduce-scatter.2.cloned.1.call-update) | async-done | bytes 163856 | tf_op jit(solution)/shard_map/reduce_scatter | solution.py:197
  468.0 1.6 add_convert_fusion.2
  (103 shorter events, 23.6 us)
Async XLA Ops:
  7.2 320.3 %copy-start = (bf16[1,384,2560]{2,1,0:T(8,128)(2,1)S(1)}, bf16[1,384,2560]{2,1,0:T(8,128)(2,1)}, u32[]{:S(2)}) copy-start(bf16[1,384,2560]{2,1,0:T(8,128)(2,1)} %param.27) | copy-start | bytes 5898244
  7.2 40.9 %all-gather.4.cloned.1.call-start = ((), (), s32[]{:S(2)}) async-start(), calls=%async_computation.5 | async-start | bytes 1392640 | tf_op jit(solution)/shard_map/all_gather | solution.py:86
  7.9 45.5 %copy-start.18 = (s32[1,64]{1,0:T(1,128)S(1)}, s32[1,64]{1,0:T(1,128)}, u32[]{:S(2)}) copy-start(s32[1,64]{1,0:T(1,128)} %param.19) | copy-start | bytes 772
  7.9 81.2 %all-gather.6.cloned.1.call-start = ((), (), s32[]{:S(2)}) async-start(), calls=%async_computation.6 | async-start | bytes 1949696 | tf_op jit(solution)/shard_map/all_gather | solution.py:91
  52.7 174.1 %all-gather.8.cloned.1.call-start = ((), (), s32[]{:S(2)}) async-start(), calls=%async_computation.7 | async-start | bytes 1392640 | tf_op jit(solution)/shard_map/all_gather | solution.py:143
  54.2 36.1 %copy-start.9 = (f32[256,64]{0,1:T(8,128)}, f32[256,64]{0,1:T(8,128)S(1)}, u32[]{:S(2)}) copy-start(f32[256,64]{0,1:T(8,128)S(1)} %get-tuple-element.12) | copy-start | bytes 196612
  54.2 36.1 %copy-start.11 = (f32[256,64]{0,1:T(8,128)}, f32[256,64]{0,1:T(8,128)S(1)}, u32[]{:S(2)}) copy-start(f32[256,64]{0,1:T(8,128)S(1)} %get-tuple-element.13) | copy-start | bytes 196612
  92.6 2.7 copy-start.2
  97.7 0.8 copy-start.10
  97.7 0.9 copy-start.12
  100.1 4.0 copy-start.4
  112.1 6.4 %copy-start.5 = (bf16[512,512]{1,0:T(8,128)(2,1)S(1)}, bf16[512,512]{1,0:T(8,128)(2,1)}, u32[]{:S(2)}) copy-start(bf16[512,512]{1,0:T(8,128)(2,1)} %get-tuple-element.9) | copy-start | bytes 1572868
  180.4 1.6 copy-start.1
  188.4 38.4 %copy-start.8 = (bf16[2560,160]{0,1:T(8,128)(2,1)S(1)}, bf16[2560,160]{0,1:T(8,128)(2,1)}, u32[]{:S(2)}) copy-start(bf16[2560,160]{0,1:T(8,128)(2,1)} %param.17) | copy-start | bytes 2457604
  188.4 38.4 %copy-start.13 = (bf16[256,160]{0,1:T(8,128)(2,1)S(1)}, bf16[256,160]{0,1:T(8,128)(2,1)}, u32[]{:S(2)}) copy-start(bf16[256,160]{0,1:T(8,128)(2,1)} %param.14) | copy-start | bytes 245764
  192.1 41.8 %copy-start.15 = (s32[256,6]{0,1:T(8,128)S(1)}, s32[256,6]{0,1:T(8,128)}, u32[]{:S(2)}) copy-start(s32[256,6]{0,1:T(8,128)} %param.22) | copy-start | bytes 18436
  228.7 25.0 %copy-start.14 = (f32[2560]{0:T(1024)S(1)}, f32[2560]{0:T(1024)}, u32[]{:S(2)}) copy-start(f32[2560]{0:T(1024)} %param.21) | copy-start | bytes 30724
  229.9 23.4 %all-to-all-start.1 = ((bf16[16,256,160]{1,2,0:T(8,128)(2,1)}), bf16[16,256,160]{1,2,0:T(8,128)(2,1)S(1)}, u32[]{:S(2)}, u32[]{:S(2)}) async-start(bf16[16,256,160]{1,2,0:T(8,128)(2,1)} %stack.2), calls=%async_computation.1 | async-start | bytes 2621440 | tf_op jit(solution)/shard_map/all_to_all | solution.py:149
  254.9 70.3 %copy-start.17 = (bf16[1,2560,768]{2,1,0:T(8,128)(2,1)S(1)}, bf16[1,2560,768]{2,1,0:T(8,128)(2,1)}, u32[]{:S(2)}) copy-start(bf16[1,2560,768]{2,1,0:T(8,128)(2,1)} %param.26) | copy-start | bytes 11796484
  330.5 7.7 %copy-start.16 = (f32[256,6]{0,1:T(8,128)S(1)}, f32[256,6]{0,1:T(8,128)}, u32[]{:S(2)}) copy-start(f32[256,6]{0,1:T(8,128)} %param.23) | copy-start | bytes 18436
  330.5 66.6 %all-to-all-start.3 = ((bf16[16,32,2560]{2,1,0:T(8,128)(2,1)}), bf16[16,32,2560]{2,1,0:T(8,128)(2,1)}, u32[]{:S(2)}, u32[]{:S(2)}) async-start(bf16[16,32,2560]{2,1,0:T(8,128)(2,1)} %bitcast.117), calls=%async_computation.3 | async-start | bytes 5242880 | tf_op jit(solution)/shard_map/all_to_all | solution.py:183
  338.1 129.9 %reduce-scatter.2.cloned.1.call-start = ((), (), s32[]{:S(2)}) async-start(), calls=%async_computation.8 | async-start | bytes 2785280 | tf_op jit(solution)/shard_map/reduce_scatter | solution.py:197
  338.3 1.5 copy-start.6
  400.1 1.2 copy-start.7
  403.6 1.2 copy-start.3
Sparse Core Ops, SparseCore 0:
  9.9 38.1 all-gather.3
  52.9 36.1 all-gather.5
  192.2 34.5 all-gather.7
  403.7 64.2 reduce-scatter.1
